TPU v7x, 512 devices: a whole 4x4x16 slice. The times are simulated.
512 devices in a mesh: wa: 32 (over x, y, core), ha: 16 (over z).
Axes of the slice: x: 4, y: 4, z: 16, core: 2. Of those that a mesh axis runs over, the one named last changes fastest.
Arguments:
- residual_in: bfloat16 [192, 16384], P('ha', 'wa'), may hold values from -43.25 to 43.25
- grad_out: bfloat16 [192, 16384], P('ha', 'wa'), may hold values from -6 to 6
- norm_gain: bfloat16 [16384], P('wa'), may hold values from 0.099609375 to 1.8984375
- w_gate: bfloat16 [16384, 26624], P('wa', 'ha'), may hold values from -0.0390625 to 0.0390625
- w_up: bfloat16 [16384, 26624], P('wa', 'ha'), may hold values from -0.0390625 to 0.0390625
- w_down: bfloat16 [26624, 16384], P('ha', 'wa'), may hold values from -0.030643146 to 0.030643146
Outputs:
- grad_in: bfloat16 [192, 16384], P('ha', 'wa')
All inputs are finite; a program needn't handle non-finite values.
Results may differ from a plain program's by a relative error of at most 0.0053.
Values may be sent and summed in bfloat16 or wider, within the bound.
No kernel may reach another device: no remote copies, remote signals or barrier semaphores. Data moves between devices by JAX's collectives and lax.ppermute only.
A program may use at most 64 MiB of HBM per device.

v0:
```python
import jax
import jax.numpy as jnp
from jax import lax
from jax.sharding import PartitionSpec as P

D = 16384


def gate_grads(gate, up, d_hidden):
    sig = jax.nn.sigmoid(gate)
    d_up = (d_hidden * gate * sig).astype(jnp.bfloat16)
    d_gate = (d_hidden * up * sig * (1.0 + gate * (1.0 - sig))).astype(jnp.bfloat16)
    return jnp.stack([d_gate, d_up])


def local(residual_in, grad_out, norm_gain, w_gate, w_up, w_down):
    stream = residual_in.astype(jnp.float32)
    squares = lax.psum(jnp.sum(stream * stream, axis=1), "wa")
    inv_rms = lax.rsqrt(squares / D + 1e-05)[:, None]
    gain_f = norm_gain.astype(jnp.float32)
    normed = (stream * inv_rms * gain_f).astype(jnp.bfloat16)
    stacked = jnp.stack([normed, grad_out])
    piece = lax.all_gather(stacked, "ha", axis=1, tiled=True)
    gate_part = jnp.dot(piece[0], w_gate, preferred_element_type=jnp.float32)
    up_part = jnp.dot(piece[0], w_up, preferred_element_type=jnp.float32)
    back_part = lax.dot_general(
        piece[1], w_down, (((1,), (1,)), ((), ())), preferred_element_type=jnp.float32
    )
    partial_sums = jnp.stack([gate_part, up_part, back_part])
    summed = lax.psum(partial_sums, "wa")
    grads = gate_grads(summed[0], summed[1], summed[2])
    total = lax.dot_general(
        grads[0], w_gate, (((1,), (1,)), ((), ())), preferred_element_type=jnp.float32
    )
    d_normed = lax.psum_scatter(
        total
        + lax.dot_general(
            grads[1], w_up, (((1,), (1,)), ((), ())), preferred_element_type=jnp.float32
        ),
        "ha",
        scatter_dimension=0,
        tiled=True,
    )
    scaled = d_normed * gain_f
    row_dot = lax.psum(jnp.sum(scaled * stream, axis=1), "wa")[:, None]
    grad_in = grad_out.astype(jnp.float32) + inv_rms * scaled - stream * inv_rms**3 * row_dot / D
    return grad_in.astype(jnp.bfloat16)


def solution(mesh):
    placed = (P("ha", "wa"), P("ha", "wa"), P("wa"), P("wa", "ha"), P("wa", "ha"), P("ha", "wa"))
    return jax.shard_map(
        local, mesh=mesh, in_specs=placed, out_specs=P("ha", "wa"), check_vma=False
    )
```

profile of v0, /device:TPU:1, one launch (start us, length us, event | category | flops | bytes accessed | tf_op | source)
XLA Modules:
  0.0 384.8 jit_solution(6059536915146214695)
XLA Ops:
  6.5 0.0 copy-start
  6.5 0.0 copy-start.2
  6.5 0.0 all-reduce.4.cloned.1.call-start
  6.5 1.0 fusion.8
  7.5 69.0 %psum.21 = f32[12]{0:T(128)S(1)} all-reduce(f32[12]{0:T(128)S(1)} %fusion.8), channel_id=1, replica_groups=mesh['wa'=32,'ha'=16] {'wa'}, use_global_device_ids=true, to_apply=%region_1.0 | all-reduce | flops 12 | bytes 96 | tf_op jit(solution)/shard_map/psum | solution.py:18
  76.5 0.7 convert_element_type.23
  77.2 0.8 fusion.16
  78.0 0.7 pad_maximum_fusion.1
  78.8 25.4 %all_gather.3 = bf16[2,192,512]{2,0,1:T(2,128)(2,1)S(1)} all-gather(bf16[2,12,512]{2,0,1:T(2,128)(2,1)S(1)} %copy.7), channel_id=1, replica_groups=mesh['wa'=32,'ha'=16] {'ha'}, dimensions={1}, use_global_device_ids=true | all-gather | bytes 417792 | tf_op jit(solution)/shard_map/all_gather | solution.py:23
  104.2 0.5 fusion.19
  104.7 0.0 copy-done.2
  104.7 0.5 convolution_bitcast_fusion.1
  105.3 0.0 copy-done
  105.3 0.0 copy-start.1
  105.3 0.5 convolution_bitcast_fusion.2
  105.8 0.9 copy-done.1
  106.7 0.7 convolution_bitcast_fusion
  107.4 2.1 pad_maximum_fusion
  109.6 0.0 all-reduce.4.cloned.1.call-update
  109.6 143.8 %all-reduce.4.cloned.1.call-done = f32[3,192,1664]{2,1,0:T(8,128)} async-done(((f32[3,192,1664]{2,1,0:T(8,128)}), f32[3,192,1664]{2,1,0:T(8,128)}) %all-reduce.4.cloned.1.call-update) | async-done | bytes 3833872 | tf_op jit(solution)/shard_map/psum | solution.py:30
  253.4 2.8 fusion.6
  256.2 0.0 copy-start.3
  256.2 0.0 copy-start.4
  256.2 3.2 convolution_add_fusion
  259.5 29.2 %fusion = f32[16,512]{1,0:T(8,128)S(1)} fusion(f32[192,512]{1,0:T(8,128)} %convolution_add_fusion), kind=kCustom, calls=%all-reduce-scatter | all-reduce-scatter fusion | flops 131073 | bytes 428032
  288.7 1.7 collective-permute-start
  290.4 2.7 collective-permute-start.1
  293.2 4.9 %collective-permute-start.2 = (f32[16,512]{1,0:T(8,128)S(1)}, f32[16,512]{1,0:T(8,128)S(1)}, u32[]{:S(2)}, u32[]{:S(2)}) collective-permute-start(f32[16,512]{1,0:T(8,128)S(1)} %fusion), channel_id=1, source_target_pairs={{0,3},{1,4},{2,5},{3,6},{4,7},{5,8},{6,9},{7,10},{8,11},{9,12},{10... | collective-permute-start | bytes 98312
  298.1 5.6 %collective-permute-start.3 = (f32[12,512]{1,0:T(8,128)S(1)}, f32[12,512]{1,0:T(8,128)S(1)}, u32[]{:S(2)}, u32[]{:S(2)}) collective-permute-start(f32[12,512]{1,0:T(8,128)S(1)} %slice.26), channel_id=1, source_target_pairs={{0,4},{1,5},{2,6},{3,7},{4,8},{5,9},{6,10},{7,11},{8,12},{9,13},{1... | collective-permute-start | bytes 73736
  303.7 1.3 dynamic-slice.4
  305.6 0.0 collective-permute-done.3
  305.6 0.0 collective-permute-done
  305.6 0.0 collective-permute-done.1
  305.6 0.0 collective-permute-done.2
  305.6 0.5 concatenate
  306.2 0.0 copy-done.3
  306.2 0.1 fusion.15
  306.3 71.0 %psum.23 = f32[12]{0:T(128)S(1)} all-reduce(f32[12]{0:T(128)S(1)} %fusion.15), channel_id=1, replica_groups=mesh['wa'=32,'ha'=16] {'wa'}, use_global_device_ids=true, to_apply=%region_5.0 | all-reduce | flops 12 | bytes 96 | tf_op jit(solution)/shard_map/psum | solution.py:45
  377.3 0.0 copy-done.4
  377.3 0.7 fusion.14
  (3 shorter events, 0.0 us)
Async XLA Ops:
  6.5 98.7 %copy-start = (bf16[512,1664]{1,0:T(8,128)(2,1)S(1)}, bf16[512,1664]{1,0:T(8,128)(2,1)}, u32[]{:S(2)}) copy-start(bf16[512,1664]{1,0:T(8,128)(2,1)} %param.9) | copy-start | bytes 5111812
  6.5 98.2 %copy-start.2 = (bf16[512,1664]{1,0:T(8,128)(2,1)S(1)}, bf16[512,1664]{1,0:T(8,128)(2,1)}, u32[]{:S(2)}) copy-start(bf16[512,1664]{1,0:T(8,128)(2,1)} %param.10) | copy-start | bytes 5111812
  6.5 246.9 %all-reduce.4.cloned.1.call-start = ((), (), s32[]{:S(2)}) async-start(), calls=%async_computation | async-start | bytes 7667712 | tf_op jit(solution)/shard_map/psum | solution.py:30
  105.3 1.5 copy-start.1
  256.2 50.0 %copy-start.3 = (bf16[12,512]{1,0:T(8,128)(2,1)S(1)}, bf16[12,512]{1,0:T(8,128)(2,1)}, u32[]{:S(2)}) copy-start(bf16[12,512]{1,0:T(8,128)(2,1)} %param.6) | copy-start | bytes 36868
  256.2 121.0 %copy-start.4 = (bf16[12,512]{1,0:T(8,128)(2,1)S(1)}, bf16[12,512]{1,0:T(8,128)(2,1)}, u32[]{:S(2)}) copy-start(bf16[12,512]{1,0:T(8,128)(2,1)} %param.7) | copy-start | bytes 36868
  288.7 16.9 %collective-permute-start = (f32[16,512]{1,0:T(8,128)S(1)}, f32[16,512]{1,0:T(8,128)S(1)}, u32[]{:S(2)}, u32[]{:S(2)}) collective-permute-start(f32[16,512]{1,0:T(8,128)S(1)} %fusion), channel_id=1, source_target_pairs={{0,1},{1,2},{2,3},{3,4},{4,5},{5,6},{6,7},{7,8},{8,9},{9,10},{10,1... | collective-permute-start | bytes 98312
  290.4 15.2 %collective-permute-start.1 = (f32[16,512]{1,0:T(8,128)S(1)}, f32[16,512]{1,0:T(8,128)S(1)}, u32[]{:S(2)}, u32[]{:S(2)}) collective-permute-start(f32[16,512]{1,0:T(8,128)S(1)} %fusion), channel_id=1, source_target_pairs={{0,2},{1,3},{2,4},{3,5},{4,6},{5,7},{6,8},{7,9},{8,10},{9,11},{10,... | collective-permute-start | bytes 98312
  293.2 12.5 %collective-permute-start.2 = (f32[16,512]{1,0:T(8,128)S(1)}, f32[16,512]{1,0:T(8,128)S(1)}, u32[]{:S(2)}, u32[]{:S(2)}) collective-permute-start(f32[16,512]{1,0:T(8,128)S(1)} %fusion), channel_id=1, source_target_pairs={{0,3},{1,4},{2,5},{3,6},{4,7},{5,8},{6,9},{7,10},{8,11},{9,12},{10... | collective-permute-start | bytes 98312
  298.1 7.5 %collective-permute-start.3 = (f32[12,512]{1,0:T(8,128)S(1)}, f32[12,512]{1,0:T(8,128)S(1)}, u32[]{:S(2)}, u32[]{:S(2)}) collective-permute-start(f32[12,512]{1,0:T(8,128)S(1)} %slice.26), channel_id=1, source_target_pairs={{0,4},{1,5},{2,6},{3,7},{4,8},{5,9},{6,10},{7,11},{8,12},{9,13},{1... | collective-permute-start | bytes 73736
Sparse Core Ops, SparseCore 0:
  109.7 143.6 all-reduce.3
where the time goes:
time: 385 us
  blocking collectives  195 us (51%)
  waiting for transfers between devices  144 us (37%)
  starting transfers between devices  14.9 us (4%)
  between operations  14.2 us (4%)
  matrix products  7.8 us (2%)
  other arithmetic  6.15 us (2%)
    psum x1, waiting for transfers between devices, local(): summed = lax.psum(partial_sums, 'wa')  144 us
    psum x1, blocking collectives, local(): row_dot = lax.psum(jnp.sum(scaled * stream, axis=1), 'wa')[:, None]  71 us
    psum x1, blocking collectives, local(): squares = lax.psum(jnp.sum(stream * stream, axis=1), 'wa')  69 us
    unnamed x1, blocking collectives  29.2 us
    all_gather x1, blocking collectives, local(): piece = lax.all_gather(stacked, 'ha', axis=1, tiled=True)  25.4 us
    unnamed x4, starting transfers between devices  14.9 us
  transfers between devices with their start and end apart: 5, of which 1 were waited for; matrix products, arithmetic and copies ran while one was open for 0% of the time, Pallas kernels for 0%

commit v1 on v0

--- a/solution.py
+++ b/solution.py
@@ -27,7 +27,9 @@
         piece[1], w_down, (((1,), (1,)), ((), ())), preferred_element_type=jnp.float32
     )
     partial_sums = jnp.stack([gate_part, up_part, back_part])
-    summed = lax.psum(partial_sums, "wa")
+    summed = partial_sums
+    for hop in (1, 2, 4, 8, 16):
+        summed = summed + lax.ppermute(summed, "wa", [(dev, dev ^ hop) for dev in range(32)])
     grads = gate_grads(summed[0], summed[1], summed[2])
     total = lax.dot_general(
         grads[0], w_gate, (((1,), (1,)), ((), ())), preferred_element_type=jnp.float32

time: 385 us -> 585 us (1.52)
  waiting for transfers between devices: 144 us -> 340 us
  starting transfers between devices: 14.9 us -> 35.7 us
  between operations: 14.2 us -> 0.89 us
    ppermute x0 -> x5, waiting for transfers between devices: none -> 340 us  [local(): lax.ppermute(summed, 'wa', [(dev, dev ^ hop) for dev in range(32)])]
    psum x1 -> x0, waiting for transfers between devices: 144 us -> none  [local(): summed = lax.psum(partial_sums, 'wa')]
    ppermute x0 -> x5, starting transfers between devices: none -> 21.7 us  [local(): lax.ppermute(summed, 'wa', [(dev, dev ^ hop) for dev in range(32)])]
  transfers between devices with their start and end apart: 5 -> 9, of which waited for: 1 -> 5; matrix products, arithmetic and copies ran while one was open for 0% -> 0% of each run, Pallas kernels for 0% -> 0%
where the time goes in v1:
time: 585 us; the launch traced here: 584 us
  waiting for transfers between devices  340 us (58%)
  blocking collectives  194 us (33%)
  starting transfers between devices  35.7 us (6%)
  other arithmetic  6.3 us (1%)
    ppermute x5, waiting for transfers between devices, local(): lax.ppermute(summed, 'wa', [(dev, dev ^ hop) for dev in range(32)])  340 us
    psum x1, blocking collectives, local(): row_dot = lax.psum(jnp.sum(scaled * stream, axis=1), 'wa')[:, None]  74.3 us
    psum x1, blocking collectives, local(): squares = lax.psum(jnp.sum(stream * stream, axis=1), 'wa')  68.9 us
    all_gather x1, blocking collectives, local(): piece = lax.all_gather(stacked, 'ha', axis=1, tiled=True)  25.4 us
    unnamed x1, blocking collectives  25.1 us
    ppermute x5, starting transfers between devices, local(): lax.ppermute(summed, 'wa', [(dev, dev ^ hop) for dev in range(32)])  21.7 us
    unnamed x4, starting transfers between devices  14 us
  transfers between devices with their start and end apart: 9, of which 5 were waited for; matrix products, arithmetic and copies ran while one was open for 0% of the time, Pallas kernels for 0%

profile of v1, /device:TPU:1, one launch (start us, length us, event | category | flops | bytes accessed | tf_op | source)
XLA Modules:
  0.0 584.2 jit_solution(12726245433025709723)
XLA Ops:
  0.0 1.0 fusion.7
  1.0 68.9 %psum.14 = f32[12]{0:T(128)S(1)} all-reduce(f32[12]{0:T(128)S(1)} %fusion.7), channel_id=1, replica_groups=mesh['wa'=32,'ha'=16] {'wa'}, use_global_device_ids=true, to_apply=%region_1.0 | all-reduce | flops 12 | bytes 96 | tf_op jit(solution)/shard_map/psum | solution.py:18
  69.8 0.7 convert_element_type.23
  70.5 0.8 fusion.15
  71.3 0.7 pad_maximum_fusion.1
  72.1 25.4 %all_gather.3 = bf16[2,192,512]{2,0,1:T(2,128)(2,1)S(1)} all-gather(bf16[2,12,512]{2,0,1:T(2,128)(2,1)S(1)} %copy.7), channel_id=1, replica_groups=mesh['wa'=32,'ha'=16] {'ha'}, dimensions={1}, use_global_device_ids=true | all-gather | bytes 417792 | tf_op jit(solution)/shard_map/all_gather | solution.py:23
  97.5 0.5 fusion.19
  98.0 0.0 copy-start.2
  98.0 0.5 convolution_bitcast_fusion.1
  98.6 0.9 copy-done.2
  99.5 0.5 convolution_bitcast_fusion.2
  100.0 0.9 copy-done.1
  100.9 0.7 convolution_bitcast_fusion
  101.7 0.2 pad_maximum_fusion
  101.9 14.0 %collective-permute-start = (f32[3,192,1664]{2,1,0:T(8,128)S(1)}, f32[3,192,1664]{2,1,0:T(8,128)S(1)}, u32[]{:S(2)}, u32[]{:S(2)}) collective-permute-start(f32[3,192,1664]{2,1,0:T(8,128)S(1)} %pad_maximum_fusion), channel_id=1, source_target_pairs={{0,16},{16,0},{32,48},{48,32},{64,80},{80,64},{96,112},{112,96},{1... | collective-permute-start | bytes 11501576 | tf_op jit(solution)/shard_map/ppermute | solution.py:32
  115.9 6.2 %collective-permute-done = f32[3,192,1664]{2,1,0:T(8,128)S(1)} collective-permute-done((f32[3,192,1664]{2,1,0:T(8,128)S(1)}, f32[3,192,1664]{2,1,0:T(8,128)S(1)}, u32[]{:S(2)}, u32[]{:S(2)}) %collective-permute-start) | collective-permute-done | bytes 3833888 | tf_op jit(solution)/shard_map/ppermute | solution.py:32
  122.2 0.4 fusion.18
  122.6 1.9 collective-permute-start.1
  124.5 84.0 %collective-permute-done.1 = f32[3,192,1664]{2,1,0:T(8,128)S(1)} collective-permute-done((f32[3,192,1664]{2,1,0:T(8,128)S(1)}, f32[3,192,1664]{2,1,0:T(8,128)S(1)}, u32[]{:S(2)}, u32[]{:S(2)}) %collective-permute-start.1) | collective-permute-done | bytes 3833888 | tf_op jit(solution)/shard_map/ppermute | solution.py:32
  208.5 0.5 fusion.25
  209.0 1.9 collective-permute-start.2
  211.0 84.6 %collective-permute-done.2 = f32[3,192,1664]{2,1,0:T(8,128)S(1)} collective-permute-done((f32[3,192,1664]{2,1,0:T(8,128)S(1)}, f32[3,192,1664]{2,1,0:T(8,128)S(1)}, u32[]{:S(2)}, u32[]{:S(2)}) %collective-permute-start.2) | collective-permute-done | bytes 3833888 | tf_op jit(solution)/shard_map/ppermute | solution.py:32
  295.6 0.4 add.39
  296.0 1.9 collective-permute-start.3
  297.9 82.3 %collective-permute-done.3 = f32[3,192,1664]{2,1,0:T(8,128)S(1)} collective-permute-done((f32[3,192,1664]{2,1,0:T(8,128)S(1)}, f32[3,192,1664]{2,1,0:T(8,128)S(1)}, u32[]{:S(2)}, u32[]{:S(2)}) %collective-permute-start.3) | collective-permute-done | bytes 3833888 | tf_op jit(solution)/shard_map/ppermute | solution.py:32
  380.2 0.4 add.40
  380.6 1.9 collective-permute-start.4
  382.5 82.9 %collective-permute-done.4 = f32[3,192,1664]{2,1,0:T(8,128)S(1)} collective-permute-done((f32[3,192,1664]{2,1,0:T(8,128)S(1)}, f32[3,192,1664]{2,1,0:T(8,128)S(1)}, u32[]{:S(2)}, u32[]{:S(2)}) %collective-permute-start.4) | collective-permute-done | bytes 3833888 | tf_op jit(solution)/shard_map/ppermute | solution.py:32
  465.5 0.4 add.41
  465.9 0.8 fusion.6
  466.6 0.0 copy-start.3
  466.6 0.0 copy-start.4
  466.6 0.8 convolution_add_fusion
  467.5 25.1 %fusion = f32[16,512]{1,0:T(8,128)S(1)} fusion(f32[192,512]{1,0:T(8,128)S(1)} %convolution_add_fusion), kind=kCustom, calls=%all-reduce-scatter | all-reduce-scatter fusion | flops 131073 | bytes 428032
  492.6 2.1 collective-permute-start.5
  494.6 1.7 collective-permute-start.6
  496.4 4.3 collective-permute-start.7
  500.7 5.9 %collective-permute-start.8 = (f32[12,512]{1,0:T(8,128)S(1)}, f32[12,512]{1,0:T(8,128)S(1)}, u32[]{:S(2)}, u32[]{:S(2)}) collective-permute-start(f32[12,512]{1,0:T(8,128)S(1)} %slice.26), channel_id=1, source_target_pairs={{0,4},{1,5},{2,6},{3,7},{4,8},{5,9},{6,10},{7,11},{8,12},{9,13},{1... | collective-permute-start | bytes 73736
  506.6 1.3 dynamic-slice.4
  508.5 0.0 collective-permute-done.8
  508.5 0.0 collective-permute-done.5
  508.5 0.0 collective-permute-done.6
  508.6 0.0 collective-permute-done.7
  508.6 0.5 concatenate
  509.1 0.1 fusion.14
  509.2 74.3 %psum.15 = f32[12]{0:T(128)S(1)} all-reduce(f32[12]{0:T(128)S(1)} %fusion.14), channel_id=1, replica_groups=mesh['wa'=32,'ha'=16] {'wa'}, use_global_device_ids=true, to_apply=%region_4.0 | all-reduce | flops 12 | bytes 96 | tf_op jit(solution)/shard_map/psum | solution.py:47
  583.5 0.0 copy-done.4
  583.5 0.7 fusion.13
  (7 shorter events, 0.1 us)
Async XLA Ops:
  0.0 98.0 %copy-start = (bf16[512,1664]{1,0:T(8,128)(2,1)S(1)}, bf16[512,1664]{1,0:T(8,128)(2,1)}, u32[]{:S(2)}) copy-start(bf16[512,1664]{1,0:T(8,128)(2,1)} %param.10) | copy-start | bytes 5111812
  98.0 1.5 copy-start.2
  99.5 1.5 copy-start.1
  101.9 20.3 %collective-permute-start = (f32[3,192,1664]{2,1,0:T(8,128)S(1)}, f32[3,192,1664]{2,1,0:T(8,128)S(1)}, u32[]{:S(2)}, u32[]{:S(2)}) collective-permute-start(f32[3,192,1664]{2,1,0:T(8,128)S(1)} %pad_maximum_fusion), channel_id=1, source_target_pairs={{0,16},{16,0},{32,48},{48,32},{64,80},{80,64},{96,112},{112,96},{1... | collective-permute-start | bytes 11501576 | tf_op jit(solution)/shard_map/ppermute | solution.py:32
  122.6 85.9 %collective-permute-start.1 = (f32[3,192,1664]{2,1,0:T(8,128)S(1)}, f32[3,192,1664]{2,1,0:T(8,128)S(1)}, u32[]{:S(2)}, u32[]{:S(2)}) collective-permute-start(f32[3,192,1664]{2,1,0:T(8,128)S(1)} %fusion.18), channel_id=1, source_target_pairs={{0,32},{16,48},{32,0},{48,16},{64,96},{80,112},{96,64},{112,80},{1... | collective-permute-start | bytes 11501576 | tf_op jit(solution)/shard_map/ppermute | solution.py:32
  209.0 86.6 %collective-permute-start.2 = (f32[3,192,1664]{2,1,0:T(8,128)S(1)}, f32[3,192,1664]{2,1,0:T(8,128)S(1)}, u32[]{:S(2)}, u32[]{:S(2)}) collective-permute-start(f32[3,192,1664]{2,1,0:T(8,128)S(1)} %fusion.25), channel_id=1, source_target_pairs={{0,64},{16,80},{32,96},{48,112},{64,0},{80,16},{96,32},{112,48},{1... | collective-permute-start | bytes 11501576 | tf_op jit(solution)/shard_map/ppermute | solution.py:32
  296.0 84.2 %collective-permute-start.3 = (f32[3,192,1664]{2,1,0:T(8,128)S(1)}, f32[3,192,1664]{2,1,0:T(8,128)S(1)}, u32[]{:S(2)}, u32[]{:S(2)}) collective-permute-start(f32[3,192,1664]{2,1,0:T(8,128)S(1)} %add.39), channel_id=1, source_target_pairs={{0,128},{16,144},{32,160},{48,176},{64,192},{80,208},{96,224},{112... | collective-permute-start | bytes 11501576 | tf_op jit(solution)/shard_map/ppermute | solution.py:32
  380.6 84.9 %collective-permute-start.4 = (f32[3,192,1664]{2,1,0:T(8,128)S(1)}, f32[3,192,1664]{2,1,0:T(8,128)S(1)}, u32[]{:S(2)}, u32[]{:S(2)}) collective-permute-start(f32[3,192,1664]{2,1,0:T(8,128)S(1)} %add.40), channel_id=1, source_target_pairs={{0,256},{16,272},{32,288},{48,304},{64,320},{80,336},{96,352},{112... | collective-permute-start | bytes 11501576 | tf_op jit(solution)/shard_map/ppermute | solution.py:32
  466.6 42.5 %copy-start.3 = (bf16[12,512]{1,0:T(8,128)(2,1)S(1)}, bf16[12,512]{1,0:T(8,128)(2,1)}, u32[]{:S(2)}) copy-start(bf16[12,512]{1,0:T(8,128)(2,1)} %param.6) | copy-start | bytes 36868
  466.6 116.9 %copy-start.4 = (bf16[12,512]{1,0:T(8,128)(2,1)S(1)}, bf16[12,512]{1,0:T(8,128)(2,1)}, u32[]{:S(2)}) copy-start(bf16[12,512]{1,0:T(8,128)(2,1)} %param.7) | copy-start | bytes 36868
  492.6 16.0 %collective-permute-start.5 = (f32[16,512]{1,0:T(8,128)S(1)}, f32[16,512]{1,0:T(8,128)S(1)}, u32[]{:S(2)}, u32[]{:S(2)}) collective-permute-start(f32[16,512]{1,0:T(8,128)S(1)} %fusion), channel_id=1, source_target_pairs={{0,1},{1,2},{2,3},{3,4},{4,5},{5,6},{6,7},{7,8},{8,9},{9,10},{10,1... | collective-permute-start | bytes 98312
  494.6 13.9 %collective-permute-start.6 = (f32[16,512]{1,0:T(8,128)S(1)}, f32[16,512]{1,0:T(8,128)S(1)}, u32[]{:S(2)}, u32[]{:S(2)}) collective-permute-start(f32[16,512]{1,0:T(8,128)S(1)} %fusion), channel_id=1, source_target_pairs={{0,2},{1,3},{2,4},{3,5},{4,6},{5,7},{6,8},{7,9},{8,10},{9,11},{10,... | collective-permute-start | bytes 98312
  496.4 12.2 %collective-permute-start.7 = (f32[16,512]{1,0:T(8,128)S(1)}, f32[16,512]{1,0:T(8,128)S(1)}, u32[]{:S(2)}, u32[]{:S(2)}) collective-permute-start(f32[16,512]{1,0:T(8,128)S(1)} %fusion), channel_id=1, source_target_pairs={{0,3},{1,4},{2,5},{3,6},{4,7},{5,8},{6,9},{7,10},{8,11},{9,12},{10... | collective-permute-start | bytes 98312
  500.7 7.8 %collective-permute-start.8 = (f32[12,512]{1,0:T(8,128)S(1)}, f32[12,512]{1,0:T(8,128)S(1)}, u32[]{:S(2)}, u32[]{:S(2)}) collective-permute-start(f32[12,512]{1,0:T(8,128)S(1)} %slice.26), channel_id=1, source_target_pairs={{0,4},{1,5},{2,6},{3,7},{4,8},{5,9},{6,10},{7,11},{8,12},{9,13},{1... | collective-permute-start | bytes 73736
